TPU v7x, 32 devices: a whole 2x2x4 slice. The times are simulated.
32 devices in a mesh: dp: 8 (over z, y), tensor: 4 (over x, core).
Axes of the slice: x: 2, y: 2, z: 4, core: 2. Of those that a mesh axis runs over, the one named last changes fastest.
Arguments:
- query: bfloat16 [384, 8192], P('dp', 'tensor'), may hold values from -128 to 128
- new_key: bfloat16 [384, 512], P('dp', 'tensor'), may hold values from -6 to 6
- new_value: bfloat16 [384, 512], P('dp', 'tensor'), may hold values from -6 to 6
- cache_key: bfloat16 [384, 128, 512], P('dp', None, 'tensor'), may hold values from -6 to 6
- cache_value: bfloat16 [384, 128, 512], P('dp', None, 'tensor'), may hold values from -6 to 6
- lengths: int32 [384], P('dp'), may hold values from 1 to 128, as said below
- hidden_in: bfloat16 [384, 4096], P(('dp', 'tensor')), may hold values from -60 to 60
- out_weight: bfloat16 [8192, 4096], P('tensor', 'dp'), may hold values from -0.0625 to 0.0625
- norm_gain: float32 [4096], replicated, may hold values from 0.25 to 1.75
- route_ids: int32 [384, 8], P(('dp', 'tensor')), may hold values from 0 to 31, all different within a row; in each aligned block of 12 rows (0 to 11, 12 to 23, ...) at most 9 rows name the same one
- route_weight: float32 [384, 8], P(('dp', 'tensor')), may hold values from 0.03 to 0.3
- w_gate: bfloat16 [32, 4096, 768], P(('dp', 'tensor')), may hold values from -0.09375 to 0.09375
- w_up: bfloat16 [32, 4096, 768], P(('dp', 'tensor')), may hold values from -0.09375 to 0.09375
- w_down: bfloat16 [32, 768, 4096], P(('dp', 'tensor')), may hold values from -0.21875 to 0.21875
Outputs:
- attended: bfloat16 [384, 4096], P(('dp', 'tensor'))
- expert_mix: bfloat16 [384, 4096], P(('dp', 'tensor'))
Inputs may be any that keep to these rules, and one draw needn't show every extreme that they name: `lengths`: row 0 holds 128 positions. `route_ids`: A row names 8 different experts. In each aligned block of 12 rows (the rows of one device along dp+tensor) no expert is named by more than 9 rows, a bound that some block reaches.
All inputs are finite; a program needn't handle non-finite values.
Results may differ from a plain program's by a relative error of at most 0.013.
Values may be sent and summed in bfloat16 or wider, within the bound.
No kernel may reach another device: no remote copies, remote signals or barrier semaphores. Data moves between devices by JAX's collectives and lax.ppermute only.
A program may use at most 128 MiB of HBM per device.

v0:
```python
import math
import jax
import jax.numpy as jnp
from jax import lax
from jax.sharding import PartitionSpec as P

HD = 128


def attend_local(query, new_key, new_value, cache_key, cache_value, lengths):
    row_count = query.shape[0]
    cache_len = cache_key.shape[1]
    kv_here = new_key.shape[1] // HD
    grouping = query.shape[1] // (kv_here * HD)
    queries = query.reshape(row_count, kv_here, grouping, HD)
    cache_keys = cache_key.reshape(row_count, cache_len, kv_here, HD)
    values = cache_value.reshape(row_count, cache_len, kv_here, HD)
    own_key = new_key.reshape(row_count, kv_here, HD)
    own_value = new_value.reshape(row_count, kv_here, HD)
    factor = 1.0 / math.sqrt(HD)
    scores = (
        jnp.einsum("rkgd,rckd->rkgc", queries, cache_keys, preferred_element_type=jnp.float32)
        * factor
    )
    own_score = (
        jnp.einsum("rkgd,rkd->rkg", queries, own_key, preferred_element_type=jnp.float32) * factor
    )
    visible = (jnp.arange(cache_len, dtype=jnp.int32)[None, :] < lengths[:, None])[:, None, None, :]
    highest = jnp.maximum(jnp.max(jnp.where(visible, scores, -1e30), axis=-1), own_score)
    exponent = jnp.where(visible, jnp.exp(scores - highest[..., None]), 0.0)
    own_exponent = jnp.exp(own_score - highest)
    totals = jnp.sum(exponent, axis=-1) + own_exponent
    probability = (exponent / totals[..., None]).astype(jnp.bfloat16)
    own_probability = (own_exponent / totals).astype(jnp.bfloat16)
    combined = jnp.einsum(
        "rkgc,rckd->rkgd", probability, values, preferred_element_type=jnp.float32
    )
    combined = (
        combined
        + own_probability.astype(jnp.float32)[..., None]
        * own_value.astype(jnp.float32)[:, :, None, :]
    )
    return combined.reshape(row_count, kv_here * grouping * HD).astype(jnp.bfloat16)


def shards(
    query,
    new_key,
    new_value,
    cache_key,
    cache_value,
    lengths,
    hidden_in,
    out_weight,
    norm_gain,
    route_ids,
    route_weight,
    w_gate,
    w_up,
    w_down,
):
    heads_out = attend_local(query, new_key, new_value, cache_key, cache_value, lengths)
    n_data = lax.axis_size("dp")
    n_heads_axis = lax.axis_size("tensor")
    tok_here = hidden_in.shape[0]
    width = hidden_in.shape[1]
    partial_cols = jnp.dot(
        lax.all_gather(heads_out, "dp", axis=0, tiled=True),
        out_weight,
        preferred_element_type=jnp.float32,
    )
    by_rows = lax.all_to_all(partial_cols, "dp", split_axis=0, concat_axis=1, tiled=True)
    summed = lax.psum_scatter(by_rows, "tensor", scatter_dimension=0, tiled=True)
    attended = (hidden_in.astype(jnp.float32) + summed).astype(jnp.bfloat16)
    widened = attended.astype(jnp.float32)
    scaled = widened * lax.rsqrt(jnp.mean(widened * widened, axis=-1, keepdims=True) + 1e-06)
    normed = (scaled * norm_gain).astype(jnp.bfloat16)
    chosen_count = route_ids.shape[1]
    experts_all = n_data * n_heads_axis
    pair_count = tok_here * chosen_count
    capacity = max(2, 3 * tok_here * chosen_count // experts_all)
    flat_ids = route_ids.reshape(pair_count)
    expert_hits = (flat_ids[:, None] == jnp.arange(experts_all, dtype=jnp.int32)[None, :]).astype(
        jnp.int32
    )
    earlier = jnp.cumsum(expert_hits, axis=0) - expert_hits
    slot_index = jnp.sum(earlier * expert_hits, axis=1)
    target = flat_ids * capacity + slot_index
    placement = (
        jnp.arange(experts_all * capacity, dtype=jnp.int32)[:, None] == target[None, :]
    ).astype(jnp.bfloat16)
    token_place = jnp.sum(placement.reshape(experts_all * capacity, tok_here, chosen_count), axis=2)
    outgoing = jnp.dot(token_place, normed, preferred_element_type=jnp.float32).astype(jnp.bfloat16)
    outgoing = outgoing.reshape(experts_all, capacity, width)
    received = lax.all_to_all(outgoing, ("dp", "tensor"), split_axis=0, concat_axis=0, tiled=True)
    flat_rows = received.reshape(-1, width)
    gate_part = jnp.dot(flat_rows, w_gate[0], preferred_element_type=jnp.float32)
    up_part = jnp.dot(flat_rows, w_up[0], preferred_element_type=jnp.float32)
    activation = (jax.nn.silu(gate_part) * up_part).astype(jnp.bfloat16)
    result = jnp.dot(activation, w_down[0], preferred_element_type=jnp.float32).astype(jnp.bfloat16)
    returned = lax.all_to_all(
        result.reshape(received.shape), ("dp", "tensor"), split_axis=0, concat_axis=0, tiled=True
    )
    returned = returned.reshape(experts_all * capacity, width)
    pair_rows = jnp.einsum("sp,sd->pd", placement, returned, preferred_element_type=jnp.float32)
    weighted = route_weight[..., None] * pair_rows.reshape(tok_here, chosen_count, width)
    expert_mix = jnp.sum(weighted, axis=1).astype(jnp.bfloat16)
    return (attended, expert_mix)


def solution(mesh):
    in_specs = (
        P("dp", "tensor"),
        P("dp", "tensor"),
        P("dp", "tensor"),
        P("dp", None, "tensor"),
        P("dp", None, "tensor"),
        P("dp"),
        P(("dp", "tensor"), None),
        P("tensor", "dp"),
        P(),
        P(("dp", "tensor"), None),
        P(("dp", "tensor"), None),
        P(("dp", "tensor"), None, None),
        P(("dp", "tensor"), None, None),
        P(("dp", "tensor"), None, None),
    )
    out_specs = (P(("dp", "tensor"), None), P(("dp", "tensor"), None))
    return jax.shard_map(shards, mesh=mesh, in_specs=in_specs, out_specs=out_specs, check_vma=False)
```

profile of v0, /device:TPU:0, one launch (start us, length us, event | category | flops | bytes accessed | tf_op | source)
XLA Modules:
  0.0 355.0 jit_solution(17587841638424498671)
XLA Ops:
  7.2 0.9 iota_compare_fusion.3
  8.1 1.0 copy.35
  9.1 0.9 fusion.39
  10.1 2.4 select_reduce_fusion
  12.9 0.6 fusion.17
  13.5 0.7 copy.40
  14.2 47.0 %all-gather.2.cloned.1.call-done = bf16[384,2048]{1,0:T(8,128)(2,1)} async-done(((bf16[48,2048]{1,0:T(8,128)(2,1)}), bf16[384,2048]{1,0:T(8,128)(2,1)}) %all-gather.2.cloned.1.call-update) | async-done | bytes 1572880 | tf_op jit(solution)/shard_map/all_gather | solution.py:68
  61.3 3.3 fusion.46
  64.6 3.7 %all-to-all-start = ((f32[8,48,512]{2,1,0:T(8,128)}), f32[8,48,512]{2,1,0:T(8,128)S(1)}, u32[]{:S(2)}, u32[]{:S(2)}) async-start(f32[8,48,512]{2,1,0:T(8,128)} %bitcast.50), calls=%async_computation | async-start | bytes 1572864 | tf_op jit(solution)/shard_map/all_to_all | solution.py:72
  68.9 18.8 %all-to-all-done = f32[8,48,512]{2,1,0:T(8,128)S(1)} async-done(((f32[8,48,512]{2,1,0:T(8,128)}), f32[8,48,512]{2,1,0:T(8,128)S(1)}, u32[]{:S(2)}, u32[]{:S(2)}) %all-to-all-start) | async-done | bytes 786464 | tf_op jit(solution)/shard_map/all_to_all | solution.py:72
  87.7 0.9 copy.34
  88.6 14.8 %fusion = f32[16,4096]{1,0:T(8,128)S(1)} fusion(f32[48,4096]{1,0:T(8,128)} %bitcast.47), kind=kCustom, calls=%all-reduce-scatter | all-reduce-scatter fusion | flops 262145 | bytes 1049088
  103.5 1.3 collective-permute-start
  106.8 2.2 convolution_convert_fusion
  109.0 4.6 %reshape.163 = bf16[32,9,4096]{2,1,0:T(8,128)(2,1)} reshape(bf16[288,4096]{1,0:T(8,128)(2,1)} %convolution_convert_fusion) | data formatting | bytes 4718592 | tf_op jit(solution)/shard_map/reshape | solution.py:94
  113.6 102.4 %all_to_all.29 = bf16[32,9,4096]{2,1,0:T(8,128)(2,1)} all-to-all(bf16[32,9,4096]{2,1,0:T(8,128)(2,1)} %reshape.163), channel_id=1, replica_groups=mesh['dp'=8,'tensor'=4] {'dp','tensor'}, dimensions={0} | all-to-all | bytes 4718592 | tf_op jit(solution)/shard_map/all_to_all | solution.py:95
  216.0 4.7 %reshape.164 = bf16[288,4096]{1,0:T(8,128)(2,1)} reshape(bf16[32,9,4096]{2,1,0:T(8,128)(2,1)} %all_to_all.29) | data formatting | bytes 4718592 | tf_op jit(solution)/shard_map/reshape | solution.py:96
  220.7 5.5 %fusion.5 = f32[288,768]{1,0:T(8,128)S(1)} fusion(bf16[288,4096]{1,0:T(8,128)(2,1)} %reshape.164, bf16[1,4096,768]{2,1,0:T(8,128)(2,1)} %param.25), kind=kOutput, calls=%fused_computation.4 | convolution fusion | flops 1811939328 | bytes 9535488 | tf_op jit(solution)/shard_map/dot_general | solution.py:97
  226.2 11.8 %fusion.7 = bf16[288,4096]{1,0:T(8,128)(2,1)} fusion(bf16[1,768,4096]{2,1,0:T(8,128)(2,1)} %param.27, bf16[288,4096]{1,0:T(8,128)(2,1)} %reshape.164, bf16[1,4096,768]{2,1,0:T(8,128)(2,1)} %param.26, f32[288,768]{1,0:T(8,128)S(1)} %fusion.5), kind=kOutput, calls=%fused_computation.6 | convolution fusion | flops 3626385408 | bytes 18186240 | tf_op jit(solution)/shard_map/dot_general | solution.py:100
  238.0 4.6 %reshape.165 = bf16[32,9,4096]{2,1,0:T(8,128)(2,1)} reshape(bf16[288,4096]{1,0:T(8,128)(2,1)} %fusion.7) | data formatting | bytes 4718592 | tf_op jit(solution)/shard_map/reshape | solution.py:102
  242.7 3.8 %all-to-all-start.2 = ((bf16[32,9,4096]{2,1,0:T(8,128)(2,1)}), bf16[32,9,4096]{2,1,0:T(8,128)(2,1)}, u32[]{:S(2)}, u32[]{:S(2)}) async-start(bf16[32,9,4096]{2,1,0:T(8,128)(2,1)} %reshape.165), calls=%async_computation.2 | async-start | bytes 8388608 | tf_op jit(solution)/shard_map/all_to_all | solution.py:101
  246.5 93.6 %all-to-all-done.2 = bf16[32,9,4096]{2,1,0:T(8,128)(2,1)} async-done(((bf16[32,9,4096]{2,1,0:T(8,128)(2,1)}), bf16[32,9,4096]{2,1,0:T(8,128)(2,1)}, u32[]{:S(2)}, u32[]{:S(2)}) %all-to-all-start.2) | async-done | bytes 2359328 | tf_op jit(solution)/shard_map/all_to_all | solution.py:101
  340.1 4.7 %reshape.169 = bf16[288,4096,1]{1,0,2:T(8,128)(2,1)} reshape(bf16[32,9,4096]{2,1,0:T(8,128)(2,1)} %all-to-all-done.2) | data formatting | bytes 4718592 | tf_op jit(solution)/shard_map/reshape | solution.py:104
  344.8 3.3 fusion.10
  (40 shorter events, 2.4 us)
Async XLA Ops:
  7.2 54.1 %copy-start = (bf16[2048,512]{1,0:T(8,128)(2,1)S(1)}, bf16[2048,512]{1,0:T(8,128)(2,1)}, u32[]{:S(2)}) copy-start(bf16[2048,512]{1,0:T(8,128)(2,1)} %param.21) | copy-start | bytes 6291460
  7.2 5.7 %copy-start.4 = (bf16[48,128]{1,0:T(8,128)(2,1)S(1)}, bf16[48,128]{1,0:T(8,128)(2,1)}, u32[]{:S(2)}) copy-start(bf16[48,128]{1,0:T(8,128)(2,1)} %param.16) | copy-start | bytes 36868
  7.2 54.1 %all-gather.2.cloned.1.call-start = ((), (), s32[]{:S(2)}) async-start(), calls=%async_computation.3 | async-start | bytes 1769472 | tf_op jit(solution)/shard_map/all_gather | solution.py:68
  7.2 5.6 %copy-start.8 = (bf16[48,128,128]{2,1,0:T(8,128)(2,1)S(1)}, bf16[48,128,128]{2,1,0:T(8,128)(2,1)}, u32[]{:S(2)}) copy-start(bf16[48,128,128]{2,1,0:T(8,128)(2,1)} %param.18) | copy-start | bytes 4718596
  14.2 54.0 %copy-start.5 = (s32[12,8]{0,1:T(8,128)S(1)}, s32[12,8]{0,1:T(8,128)}, u32[]{:S(2)}) copy-start(s32[12,8]{0,1:T(8,128)} %param.23) | copy-start | bytes 1156
  64.6 40.3 %copy-start.7 = (u32[32]{0:T(128)S(1)}, u32[32]{0:T(128)}, u32[]{:S(2)}) copy-start(u32[32]{0:T(128)} %constant.35) | copy-start | bytes 388
  64.6 23.1 %all-to-all-start = ((f32[8,48,512]{2,1,0:T(8,128)}), f32[8,48,512]{2,1,0:T(8,128)S(1)}, u32[]{:S(2)}, u32[]{:S(2)}) async-start(f32[8,48,512]{2,1,0:T(8,128)} %bitcast.50), calls=%async_computation | async-start | bytes 1572864 | tf_op jit(solution)/shard_map/all_to_all | solution.py:72
  68.3 38.3 %copy-start.2 = (bf16[12,4096]{1,0:T(8,128)(2,1)S(1)}, bf16[12,4096]{1,0:T(8,128)(2,1)}, u32[]{:S(2)}) copy-start(bf16[12,4096]{1,0:T(8,128)(2,1)} %param.20) | copy-start | bytes 294916
  87.7 19.1 %copy-start.3 = (f32[4096]{0:T(1024)S(1)}, f32[4096]{0:T(1024)}, u32[]{:S(2)}) copy-start(f32[4096]{0:T(1024)} %param.22) | copy-start | bytes 49156
  103.5 2.7 collective-permute-start
  106.7 6.9 %copy-start.1 = (bf16[12,4096]{1,0:T(8,128)(2,1)}, bf16[12,4096]{1,0:T(8,128)(2,1)S(1)}, u32[]{:S(2)}) copy-start(bf16[12,4096]{1,0:T(8,128)(2,1)S(1)} %get-tuple-element.3) | copy-start | bytes 294916
  242.7 3.8 %copy-start.6 = (f32[12,8]{0,1:T(8,128)S(1)}, f32[12,8]{0,1:T(8,128)}, u32[]{:S(2)}) copy-start(f32[12,8]{0,1:T(8,128)} %param.24) | copy-start | bytes 1156
  242.7 97.5 %all-to-all-start.2 = ((bf16[32,9,4096]{2,1,0:T(8,128)(2,1)}), bf16[32,9,4096]{2,1,0:T(8,128)(2,1)}, u32[]{:S(2)}, u32[]{:S(2)}) async-start(bf16[32,9,4096]{2,1,0:T(8,128)(2,1)} %reshape.165), calls=%async_computation.2 | async-start | bytes 8388608 | tf_op jit(solution)/shard_map/all_to_all | solution.py:101
Sparse Core Ops, SparseCore 0:
  14.3 46.8 all-gather.1
where the time goes:
time: 356 us; the launch traced here: 355 us
  waiting for transfers between devices  159 us (45%)
  blocking collectives  117 us (33%)
  matrix products  30.1 us (8%)
  local copies, waits for them, and re-layouts  22.6 us (6%)
  between operations  14.9 us (4%)
  starting transfers between devices  8.81 us (2%)
    all_to_all x1, blocking collectives, shards(): lax.all_to_all(outgoing, ('dp', 'tensor'), split_axis=0, concat_axis=0, t...  102 us
    all_to_all x1, waiting for transfers between devices, shards(): lax.all_to_all(result.reshape(received.shape), ('dp', 'tensor'), split_ax...  93.6 us
    all_gather x1, waiting for transfers between devices, shards(): lax.all_gather(heads_out, 'dp', axis=0, tiled=True)  47 us
    all_to_all x1, waiting for transfers between devices, shards(): lax.all_to_all(partial_cols, 'dp', split_axis=0, concat_axis=1, tiled=True)  18.8 us
    unnamed x1, blocking collectives  14.8 us
    dot_general x1, matrix products, shards(): jnp.dot(activation, w_down[0], preferred_element_type=jnp.float32)  11.8 us
  transfers between devices with their start and end apart: 4, of which 3 were waited for; matrix products, arithmetic and copies ran while one was open for 0% of the time, Pallas kernels for 0%

commit v1 on v0

--- a/solution.py
+++ b/solution.py
@@ -69,7 +69,19 @@
         out_weight,
         preferred_element_type=jnp.float32,
     )
-    by_rows = lax.all_to_all(partial_cols, "dp", split_axis=0, concat_axis=1, tiled=True)
+    ways, here = (lax.axis_size("dp"), lax.axis_index("dp"))
+    width_2 = partial_cols.shape[0] // ways
+    shape = list(partial_cols.shape)
+    shape[0] = width_2
+    height = shape[1]
+    shape[1] = height * ways
+    full = jnp.zeros(shape, partial_cols.dtype)
+    for mask in range(ways):
+        part = lax.dynamic_slice_in_dim(partial_cols, (here ^ mask) * width_2, width_2, axis=0)
+        if mask:
+            part = lax.ppermute(part, "dp", [(d, d ^ mask) for d in range(ways)])
+        full = lax.dynamic_update_slice_in_dim(full, part, (here ^ mask) * height, axis=1)
+    by_rows = full
     summed = lax.psum_scatter(by_rows, "tensor", scatter_dimension=0, tiled=True)
     attended = (hidden_in.astype(jnp.float32) + summed).astype(jnp.bfloat16)
     widened = attended.astype(jnp.float32)

time: 356 us -> 352 us (0.989)
  waiting for transfers between devices: 159 us -> 148 us
  starting transfers between devices: 8.81 us -> 16.4 us
    all_to_all x1 -> x0, waiting for transfers between devices: 18.8 us -> none  [shards(): lax.all_to_all(partial_cols, 'dp', split_axis=0, concat_axis=1, tiled=True)]
    ppermute x0 -> x7, starting transfers between devices: none -> 11.3 us  [shards(): part = lax.ppermute(part, 'dp', [(d, d ^ mask) for d in range(ways)])]
    ppermute x0 -> x7, waiting for transfers between devices: none -> 7.44 us  [shards(): part = lax.ppermute(part, 'dp', [(d, d ^ mask) for d in range(ways)])]
    all_to_all x1 -> x0, starting transfers between devices: 3.68 us -> none  [shards(): lax.all_to_all(partial_cols, 'dp', split_axis=0, concat_axis=1, tiled=True)]
  transfers between devices with their start and end apart: 4 -> 10, of which waited for: 3 -> 4; matrix products, arithmetic and copies ran while one was open for 0% -> 1% of each run, Pallas kernels for 0% -> 0%
where the time goes in v1:
time: 352 us; the launch traced here: 351 us
  waiting for transfers between devices  148 us (42%)
  blocking collectives  118 us (34%)
  matrix products  29.2 us (8%)
  local copies, waits for them, and re-layouts  23.5 us (7%)
  starting transfers between devices  16.4 us (5%)
  between operations  15.1 us (4%)
    all_to_all x1, blocking collectives, shards(): lax.all_to_all(outgoing, ('dp', 'tensor'), split_axis=0, concat_axis=0, t...  103 us
    all_to_all x1, waiting for transfers between devices, shards(): lax.all_to_all(result.reshape(received.shape), ('dp', 'tensor'), split_ax...  93.6 us
    all_gather x1, waiting for transfers between devices, shards(): lax.all_gather(heads_out, 'dp', axis=0, tiled=True)  46.6 us
    unnamed x1, blocking collectives  14.3 us
    dot_general x1, matrix products, shards(): jnp.dot(activation, w_down[0], preferred_element_type=jnp.float32)  11.8 us
    ppermute x7, starting transfers between devices, shards(): part = lax.ppermute(part, 'dp', [(d, d ^ mask) for d in range(ways)])  11.3 us
    ppermute x7, waiting for transfers between devices, shards(): part = lax.ppermute(part, 'dp', [(d, d ^ mask) for d in range(ways)])  7.44 us
  transfers between devices with their start and end apart: 10, of which 4 were waited for; matrix products, arithmetic and copies ran while one was open for 1% of the time, Pallas kernels for 0%

profile of v1, /device:TPU:0, one launch (start us, length us, event | category | flops | bytes accessed | tf_op | source)
XLA Modules:
  0.0 351.3 jit_solution(13287293192389831828)
XLA Ops:
  10.1 2.4 select_reduce_fusion
  14.8 46.6 %all-gather.2.cloned.1.call-done = bf16[384,2048]{1,0:T(8,128)(2,1)} async-done(((bf16[48,2048]{1,0:T(8,128)(2,1)}), bf16[384,2048]{1,0:T(8,128)(2,1)}) %all-gather.2.cloned.1.call-update) | async-done | bytes 1572880 | tf_op jit(solution)/shard_map/all_gather | solution.py:68
  61.3 2.4 fusion.46
  65.3 1.5 collective-permute-start.1
  66.8 1.5 collective-permute-start.2
  68.3 1.7 collective-permute-start.3
  70.0 1.2 collective-permute-start.4
  71.3 1.7 collective-permute-start.5
  73.8 3.1 collective-permute-start.6
  77.0 5.4 %collective-permute-done.3 = f32[48,512]{1,0:T(8,128)S(1)} collective-permute-done((f32[48,512]{1,0:T(8,128)S(1)}, f32[48,512]{1,0:T(8,128)S(1)}, u32[]{:S(2)}, u32[]{:S(2)}) %collective-permute-start.3) | collective-permute-done | bytes 98336 | tf_op jit(solution)/shard_map/ppermute | solution.py:82
  82.4 2.1 collective-permute-done.4
  84.5 14.3 %fusion = f32[16,4096]{1,0:T(8,128)S(1)} fusion(f32[48,4096]{1,0:T(8,128)S(1)} %constant_dynamic-update-slice_fusion), kind=kCustom, calls=%all-reduce-scatter | all-reduce-scatter fusion | flops 262145 | bytes 1049088
  98.9 1.3 collective-permute-start.7
  102.1 2.3 convolution_convert_fusion
  104.4 4.6 %reshape.160 = bf16[32,9,4096]{2,1,0:T(8,128)(2,1)} reshape(bf16[288,4096]{1,0:T(8,128)(2,1)} %convolution_convert_fusion) | data formatting | bytes 4718592 | tf_op jit(solution)/shard_map/reshape | solution.py:106
  109.0 103.3 %all_to_all.10 = bf16[32,9,4096]{2,1,0:T(8,128)(2,1)} all-to-all(bf16[32,9,4096]{2,1,0:T(8,128)(2,1)} %reshape.160), channel_id=1, replica_groups=mesh['dp'=8,'tensor'=4] {'dp','tensor'}, dimensions={0} | all-to-all | bytes 4718592 | tf_op jit(solution)/shard_map/all_to_all | solution.py:107
  212.3 4.7 %reshape.161 = bf16[288,4096]{1,0:T(8,128)(2,1)} reshape(bf16[32,9,4096]{2,1,0:T(8,128)(2,1)} %all_to_all.10) | data formatting | bytes 4718592 | tf_op jit(solution)/shard_map/reshape | solution.py:108
  217.0 5.5 %fusion.5 = f32[288,768]{1,0:T(8,128)S(1)} fusion(bf16[288,4096]{1,0:T(8,128)(2,1)} %reshape.161, bf16[1,4096,768]{2,1,0:T(8,128)(2,1)} %param.25), kind=kOutput, calls=%fused_computation.4 | convolution fusion | flops 1811939328 | bytes 9535488 | tf_op jit(solution)/shard_map/dot_general | solution.py:109
  222.5 11.8 %fusion.7 = bf16[288,4096]{1,0:T(8,128)(2,1)} fusion(bf16[1,768,4096]{2,1,0:T(8,128)(2,1)} %param.27, bf16[288,4096]{1,0:T(8,128)(2,1)} %reshape.161, bf16[1,4096,768]{2,1,0:T(8,128)(2,1)} %param.26, f32[288,768]{1,0:T(8,128)S(1)} %fusion.5), kind=kOutput, calls=%fused_computation.6 | convolution fusion | flops 3626385408 | bytes 18186240 | tf_op jit(solution)/shard_map/dot_general | solution.py:112
  234.4 4.6 %reshape.162 = bf16[32,9,4096]{2,1,0:T(8,128)(2,1)} reshape(bf16[288,4096]{1,0:T(8,128)(2,1)} %fusion.7) | data formatting | bytes 4718592 | tf_op jit(solution)/shard_map/reshape | solution.py:114
  239.0 3.8 %all-to-all-start.1 = ((bf16[32,9,4096]{2,1,0:T(8,128)(2,1)}), bf16[32,9,4096]{2,1,0:T(8,128)(2,1)}, u32[]{:S(2)}, u32[]{:S(2)}) async-start(bf16[32,9,4096]{2,1,0:T(8,128)(2,1)} %reshape.162), calls=%async_computation.1 | async-start | bytes 8388608 | tf_op jit(solution)/shard_map/all_to_all | solution.py:113
  242.9 93.6 %all-to-all-done.1 = bf16[32,9,4096]{2,1,0:T(8,128)(2,1)} async-done(((bf16[32,9,4096]{2,1,0:T(8,128)(2,1)}), bf16[32,9,4096]{2,1,0:T(8,128)(2,1)}, u32[]{:S(2)}, u32[]{:S(2)}) %all-to-all-start.1) | async-done | bytes 2359328 | tf_op jit(solution)/shard_map/all_to_all | solution.py:113
  336.5 4.7 %reshape.166 = bf16[288,4096,1]{1,0,2:T(8,128)(2,1)} reshape(bf16[32,9,4096]{2,1,0:T(8,128)(2,1)} %all-to-all-done.1) | data formatting | bytes 4718592 | tf_op jit(solution)/shard_map/reshape | solution.py:116
  341.2 3.3 fusion.10
  (60 shorter events, 8.9 us)
Async XLA Ops:
  7.2 54.1 %copy-start = (bf16[2048,512]{1,0:T(8,128)(2,1)S(1)}, bf16[2048,512]{1,0:T(8,128)(2,1)}, u32[]{:S(2)}) copy-start(bf16[2048,512]{1,0:T(8,128)(2,1)} %param.21) | copy-start | bytes 6291460
  7.2 5.7 %copy-start.4 = (bf16[48,128]{1,0:T(8,128)(2,1)S(1)}, bf16[48,128]{1,0:T(8,128)(2,1)}, u32[]{:S(2)}) copy-start(bf16[48,128]{1,0:T(8,128)(2,1)} %param.16) | copy-start | bytes 36868
  7.2 54.1 %all-gather.2.cloned.1.call-start = ((), (), s32[]{:S(2)}) async-start(), calls=%async_computation.2 | async-start | bytes 1769472 | tf_op jit(solution)/shard_map/all_gather | solution.py:68
  7.2 5.6 %copy-start.8 = (bf16[48,128,128]{2,1,0:T(8,128)(2,1)S(1)}, bf16[48,128,128]{2,1,0:T(8,128)(2,1)}, u32[]{:S(2)}) copy-start(bf16[48,128,128]{2,1,0:T(8,128)(2,1)} %param.18) | copy-start | bytes 4718596
  12.5 1.8 copy-start.5
  63.8 36.4 %copy-start.7 = (u32[32]{0:T(128)S(1)}, u32[32]{0:T(128)}, u32[]{:S(2)}) copy-start(u32[32]{0:T(128)} %constant.64) | copy-start | bytes 388
  64.5 37.4 %copy-start.2 = (bf16[12,4096]{1,0:T(8,128)(2,1)S(1)}, bf16[12,4096]{1,0:T(8,128)(2,1)}, u32[]{:S(2)}) copy-start(bf16[12,4096]{1,0:T(8,128)(2,1)} %param.20) | copy-start | bytes 294916
  64.5 37.6 %copy-start.3 = (f32[4096]{0:T(1024)S(1)}, f32[4096]{0:T(1024)}, u32[]{:S(2)}) copy-start(f32[4096]{0:T(1024)} %param.22) | copy-start | bytes 49156
  64.5 6.7 %collective-permute-start = (f32[48,512]{1,0:T(8,128)}, f32[48,512]{1,0:T(8,128)}, u32[]{:S(2)}, u32[]{:S(2)}) collective-permute-start(f32[48,512]{1,0:T(8,128)} %get-tuple-element.10), channel_id=1, source_target_pairs={{0,4},{4,0},{8,12},{12,8},{16,20},{20,16},{24,28},{28,24},{1,5},{5... | collective-permute-start | bytes 294920 | tf_op jit(solution)/shard_map/ppermute | solution.py:82
  65.3 8.5 %collective-permute-start.1 = (f32[48,512]{1,0:T(8,128)}, f32[48,512]{1,0:T(8,128)S(1)}, u32[]{:S(2)}, u32[]{:S(2)}) collective-permute-start(f32[48,512]{1,0:T(8,128)} %get-tuple-element.9), channel_id=1, source_target_pairs={{0,8},{4,12},{8,0},{12,4},{16,24},{20,28},{24,16},{28,20},{1,9},{5... | collective-permute-start | bytes 294920 | tf_op jit(solution)/shard_map/ppermute | solution.py:82
  66.8 10.1 %collective-permute-start.2 = (f32[48,512]{1,0:T(8,128)}, f32[48,512]{1,0:T(8,128)S(1)}, u32[]{:S(2)}, u32[]{:S(2)}) collective-permute-start(f32[48,512]{1,0:T(8,128)} %get-tuple-element.8), channel_id=1, source_target_pairs={{0,12},{4,8},{8,4},{12,0},{16,28},{20,24},{24,20},{28,16},{1,13},{... | collective-permute-start | bytes 294920 | tf_op jit(solution)/shard_map/ppermute | solution.py:82
  68.3 14.0 %collective-permute-start.3 = (f32[48,512]{1,0:T(8,128)S(1)}, f32[48,512]{1,0:T(8,128)S(1)}, u32[]{:S(2)}, u32[]{:S(2)}) collective-permute-start(f32[48,512]{1,0:T(8,128)S(1)} %get-tuple-element.7), channel_id=1, source_target_pairs={{0,16},{4,20},{8,24},{12,28},{16,0},{20,4},{24,8},{28,12},{1,17},{... | collective-permute-start | bytes 294920 | tf_op jit(solution)/shard_map/ppermute | solution.py:82
  70.0 14.4 %collective-permute-start.4 = (f32[48,512]{1,0:T(8,128)S(1)}, f32[48,512]{1,0:T(8,128)S(1)}, u32[]{:S(2)}, u32[]{:S(2)}) collective-permute-start(f32[48,512]{1,0:T(8,128)S(1)} %get-tuple-element.6), channel_id=1, source_target_pairs={{0,20},{4,16},{8,28},{12,24},{16,4},{20,0},{24,12},{28,8},{1,21},{... | collective-permute-start | bytes 294920 | tf_op jit(solution)/shard_map/ppermute | solution.py:82
  71.3 13.2 %collective-permute-start.5 = (f32[48,512]{1,0:T(8,128)S(1)}, f32[48,512]{1,0:T(8,128)S(1)}, u32[]{:S(2)}, u32[]{:S(2)}) collective-permute-start(f32[48,512]{1,0:T(8,128)S(1)} %get-tuple-element.5), channel_id=1, source_target_pairs={{0,24},{4,28},{8,16},{12,20},{16,8},{20,12},{24,0},{28,4},{1,25},{... | collective-permute-start | bytes 294920 | tf_op jit(solution)/shard_map/ppermute | solution.py:82
  73.8 10.7 %collective-permute-start.6 = (f32[48,512]{1,0:T(8,128)S(1)}, f32[48,512]{1,0:T(8,128)S(1)}, u32[]{:S(2)}, u32[]{:S(2)}) collective-permute-start(f32[48,512]{1,0:T(8,128)S(1)} %get-tuple-element.4), channel_id=1, source_target_pairs={{0,28},{4,24},{8,20},{12,16},{16,12},{20,8},{24,4},{28,0},{1,29},{... | collective-permute-start | bytes 294920 | tf_op jit(solution)/shard_map/ppermute | solution.py:82
  98.9 2.7 collective-permute-start.7
  102.1 6.9 %copy-start.1 = (bf16[12,4096]{1,0:T(8,128)(2,1)}, bf16[12,4096]{1,0:T(8,128)(2,1)S(1)}, u32[]{:S(2)}) copy-start(bf16[12,4096]{1,0:T(8,128)(2,1)S(1)} %get-tuple-element.3) | copy-start | bytes 294916
  239.0 3.8 %copy-start.6 = (f32[12,8]{0,1:T(8,128)S(1)}, f32[12,8]{0,1:T(8,128)}, u32[]{:S(2)}) copy-start(f32[12,8]{0,1:T(8,128)} %param.24) | copy-start | bytes 1156
  239.0 97.5 %all-to-all-start.1 = ((bf16[32,9,4096]{2,1,0:T(8,128)(2,1)}), bf16[32,9,4096]{2,1,0:T(8,128)(2,1)}, u32[]{:S(2)}, u32[]{:S(2)}) async-start(bf16[32,9,4096]{2,1,0:T(8,128)(2,1)} %reshape.162), calls=%async_computation.1 | async-start | bytes 8388608 | tf_op jit(solution)/shard_map/all_to_all | solution.py:113
Sparse Core Ops, SparseCore 0:
  14.4 46.8 all-gather.1
